TPU v7x, 32 devices: a whole 2x2x4 slice. The times are simulated.
32 devices in a mesh: snp: 8 (over z, y), ind: 4 (over x, core).
Axes of the slice: x: 2, y: 2, z: 4, core: 2. Of those that a mesh axis runs over, the one named last changes fastest.
Arguments:
- beta_hat: float32 [64, 8192], P('ind', 'snp'), may hold values from -8 to 8
- ld_band: float32 [8192, 1024], P('snp'), as said below
- band_start: int32 [64], P('snp'), may hold values from -480 to 7648, as said below
- heritability: float32 [64], P('ind'), may hold values from 0.2 to 0.6
- genotypes: bfloat16 [4096, 8192], P('ind', 'snp'), may hold values from 0 to 2, as said below
Outputs:
- weights: float32 [64, 8192], P('ind', 'snp')
- scores: float32 [64, 4096], P(None, ('ind', 'snp'))
Inputs may be any that keep to these rules, and one draw needn't show every extreme that they name: ld_band is a symmetric matrix R in band form: entry k of row i is R[i, band_start[i // 128] + k]; R[i, i] = 1; R[i, j] = 0 when |i - j| > 416 or j lies outside the SNPs; the off-diagonal magnitudes of a row sum to 2.5 at most. `band_start`: block b's window starts at 128 * b - 416 - k with k from 0 to 64; the first block has k = 64 and the last block k = 0. `genotypes`: dosages are 0, 1 or 2.
All inputs are finite; a program needn't handle non-finite values.
Results may differ from a plain program's by a relative error of at most 0.0021.
Values may be sent and summed in bfloat16 or wider, within the bound.
No kernel may reach another device: no remote copies, remote signals or barrier semaphores. Data moves between devices by JAX's collectives and lax.ppermute only.
A program may use at most 64 MiB of HBM per device.

v0:
```python
import jax
import jax.numpy as jnp
from jax import lax
from jax.sharding import PartitionSpec as P

BLK = 128
ITERS = 2
M_GENOME = 1100000
N_GWAS = 1000000


def padded_2(block, sides, width):
    for axis, dim in sides:
        count = lax.axis_size(axis)
        forward = [(i, i + 1) for i in range(count - 1)]
        backward = [(target, source) for source, target in forward]
        low = lax.ppermute(
            lax.slice_in_dim(block, block.shape[dim] - width, None, axis=dim), axis, forward
        )
        high = lax.ppermute(lax.slice_in_dim(block, 0, width, axis=dim), axis, backward)
        block = jnp.concatenate([low, block, high], axis=dim)
    return block


def apply_operator(vector, ld_band, band_start, ridge_shift):
    band_cols = ld_band.shape[1]
    halo_cols = band_cols - BLK
    padded = padded_2(vector, (("snp", 1),), halo_cols)
    local_rows = vector.shape[1]
    offsets = band_start - lax.axis_index("snp") * local_rows + halo_cols
    windows = jax.vmap(lambda row_begin: lax.dynamic_slice_in_dim(padded, row_begin, band_cols, 1))(
        offsets
    )
    blocks = ld_band.reshape(band_start.shape[0], BLK, band_cols)
    product = jnp.einsum("btk,brk->tbr", windows, blocks, precision=lax.Precision.HIGHEST)
    return product.reshape(vector.shape) + ridge_shift[:, None] * vector


def paired_sums(residual, product):
    return lax.psum(
        (jnp.sum(residual * residual, axis=1), jnp.sum(residual * product, axis=1)), "snp"
    )


def local(beta_hat, ld_band, band_start, heritability, genotypes):
    ridge_shift = M_GENOME / N_GWAS / heritability
    weights = jnp.zeros_like(beta_hat)
    residual = beta_hat
    product = apply_operator(residual, ld_band, band_start, ridge_shift)
    norm_now, mixed = paired_sums(residual, product)
    step_size = norm_now / mixed
    direction = residual
    along = product
    for turn_index in range(ITERS):
        weights = weights + step_size[:, None] * direction
        residual = residual - step_size[:, None] * along
        if turn_index + 1 < ITERS:
            product = apply_operator(residual, ld_band, band_start, ridge_shift)
            norm_next, mixed = paired_sums(residual, product)
            ratio_new = norm_next / norm_now
            step_size = norm_next / (mixed - ratio_new * norm_next / step_size)
            direction = residual + ratio_new[:, None] * direction
            along = product + ratio_new[:, None] * along
            norm_now = norm_next
    rounded = weights.astype(jnp.bfloat16)
    partial_scores = lax.dot_general(
        lax.all_gather(rounded, "ind", axis=0, tiled=True),
        genotypes,
        (((1,), (1,)), ((), ())),
        preferred_element_type=jnp.float32,
    )
    complete = lax.psum(partial_scores, "snp")
    count = complete.shape[1] * lax.axis_size("ind")
    summed = lax.psum(jnp.sum(complete, axis=1), "ind")
    average = summed / count
    centred = complete - average[:, None]
    variance = lax.psum(jnp.sum(centred * centred, axis=1), "ind") / count
    share_cols = complete.shape[1] // lax.axis_size("snp")
    own_part = lax.dynamic_slice_in_dim(centred, lax.axis_index("snp") * share_cols, share_cols, 1)
    scores = own_part * lax.rsqrt(variance + 1e-05)[:, None]
    return (weights, scores)


def solution(mesh):
    placed = (P("ind", "snp"), P("snp", None), P("snp"), P("ind"), P("ind", "snp"))
    return jax.shard_map(
        local,
        mesh=mesh,
        in_specs=placed,
        out_specs=(P("ind", "snp"), P(None, ("ind", "snp"))),
        check_vma=False,
    )
```

profile of v0, /device:TPU:0, one launch (start us, length us, event | category | flops | bytes accessed | tf_op | source)
XLA Modules:
  0.0 196.7 jit_solution(16912710394377717429)
XLA Ops:
  7.2 1.0 fusion.5
  8.2 4.9 %collective-permute-start = (f32[16,896]{1,0:T(8,128)S(1)}, f32[16,896]{1,0:T(8,128)S(1)}, u32[]{:S(2)}, u32[]{:S(2)}) collective-permute-start(f32[16,896]{1,0:T(8,128)S(1)} %get-tuple-element.50), channel_id=1, source_target_pairs={{0,4},{4,8},{8,12},{12,16},{16,20},{20,24},{24,28},{1,5},{5,9},{9,... | collective-permute-start | bytes 172040 | tf_op jit(solution)/shard_map/ppermute | solution.py:17
  13.1 1.3 collective-permute-start.1
  15.8 3.4 %collective-permute-done.1 = f32[16,896]{1,0:T(8,128)S(1)} collective-permute-done((f32[16,896]{1,0:T(8,128)S(1)}, f32[16,896]{1,0:T(8,128)S(1)}, u32[]{:S(2)}, u32[]{:S(2)}) %collective-permute-start.1) | collective-permute-done | bytes 57376 | tf_op jit(solution)/shard_map/ppermute | solution.py:20
  19.2 0.9 pad_maximum_fusion
  20.1 10.6 %while.2 = (s32[]{:T(128)}, f32[16,2816]{1,0:T(8,128)S(1)}, s32[8,2]{0,1:T(2,128)S(1)}, f32[8,16,1024]{2,1,0:T(8,128)S(1)}, s32[]{:T(128)}) while((s32[]{:T(128)}, f32[16,2816]{1,0:T(8,128)S(1)}, s32[8,2]{0,1:T(2,128)S(1)}, f32[8,16,1024]{2,1,0:T(8,128)S(1)}, s32[]{:T(128)}) %tuple.38), condition=%wide.while_cond, body=%wide.while_body.sunk | while | flops 2 | bytes 131169 | solution.py:31
  20.7 0.7 bitcast_dynamic-update-slice_fusion.4
  22.0 0.7 bitcast_dynamic-update-slice_fusion.4
  23.4 0.7 bitcast_dynamic-update-slice_fusion.4
  24.7 0.7 bitcast_dynamic-update-slice_fusion.4
  26.0 0.7 bitcast_dynamic-update-slice_fusion.4
  27.3 0.7 bitcast_dynamic-update-slice_fusion.4
  28.7 0.7 bitcast_dynamic-update-slice_fusion.4
  30.0 0.7 bitcast_dynamic-update-slice_fusion.4
  30.7 5.3 %convolution_bitcast_fusion.1 = f32[8,2,8,128]{3,2,1,0:T(8,128)S(1)} fusion(f32[8,16,1024]{2,1,0:T(8,128)S(1)} %get-tuple-element.9, f32[8,128,1024]{2,1,0:T(8,128)} %bitcast.41), kind=kOutput, calls=%fused_computation.5 | convolution fusion | flops 201326592 | bytes 4784128 | tf_op jit(solution)/shard_map/btk,brk->tbr/dot_general | solution.py:35
  36.2 19.8 %all-reduce.2 = (f32[16]{0:T(128)S(1)}, f32[16]{0:T(128)S(1)}) all-reduce(f32[16]{0:T(128)S(1)} %get-tuple-element.21, f32[16]{0:T(128)S(1)} %get-tuple-element.20), channel_id=1, replica_groups=mesh['snp'=8,'ind'=4] {'snp'}, use_global_device_ids=true, to_apply=%region_1.0 | all-reduce | flops 32 | bytes 256 | tf_op jit(solution)/shard_map/psum | solution.py:40
  56.2 1.6 collective-permute-start.2
  57.8 1.3 collective-permute-start.3
  59.6 4.3 %collective-permute-done.3 = f32[16,896]{1,0:T(8,128)S(1)} collective-permute-done((f32[16,896]{1,0:T(8,128)S(1)}, f32[16,896]{1,0:T(8,128)S(1)}, u32[]{:S(2)}, u32[]{:S(2)}) %collective-permute-start.3) | collective-permute-done | bytes 57376 | tf_op jit(solution)/shard_map/ppermute | solution.py:20
  63.9 10.6 %while.3 = (s32[]{:T(128)}, f32[16,2816]{1,0:T(8,128)S(1)}, s32[8,2]{0,1:T(2,128)S(1)}, f32[8,16,1024]{2,1,0:T(8,128)S(1)}, s32[]{:T(128)}) while((s32[]{:T(128)}, f32[16,2816]{1,0:T(8,128)S(1)}, s32[8,2]{0,1:T(2,128)S(1)}, f32[8,16,1024]{2,1,0:T(8,128)S(1)}, s32[]{:T(128)}) %tuple.46), condition=%wide.while_cond.1, body=%wide.while_body.1.sunk | while | flops 2 | bytes 131169 | solution.py:31
  64.5 0.7 bitcast_dynamic-update-slice_fusion.5
  65.8 0.7 bitcast_dynamic-update-slice_fusion.5
  72.5 0.7 bitcast_dynamic-update-slice_fusion.5
  74.5 5.3 %convolution_bitcast_fusion = f32[8,2,8,128]{3,2,1,0:T(8,128)S(1)} fusion(f32[8,16,1024]{2,1,0:T(8,128)S(1)} %get-tuple-element.17, f32[8,128,1024]{2,1,0:T(8,128)} %bitcast.42), kind=kOutput, calls=%fused_computation.4 | convolution fusion | flops 201326592 | bytes 4784128 | tf_op jit(solution)/shard_map/btk,brk->tbr/dot_general | solution.py:35
  80.0 18.6 %all-reduce.1 = (f32[16]{0:T(128)S(1)}, f32[16]{0:T(128)S(1)}) all-reduce(f32[16]{0:T(128)S(1)} %get-tuple-element.19, f32[16]{0:T(128)S(1)} %get-tuple-element.18), channel_id=1, replica_groups=mesh['snp'=8,'ind'=4] {'snp'}, use_global_device_ids=true, to_apply=%region_5.0 | all-reduce | flops 32 | bytes 256 | tf_op jit(solution)/shard_map/psum | solution.py:40
  99.3 5.4 %all_gather.3 = bf16[64,1024]{1,0:T(8,128)(2,1)S(1)} all-gather(bf16[16,1024]{1,0:T(8,128)(2,1)S(1)} %get-tuple-element.44), channel_id=1, replica_groups=mesh['snp'=8,'ind'=4] {'ind'}, dimensions={0}, use_global_device_ids=true | all-gather | bytes 163840 | tf_op jit(solution)/shard_map/all_gather | solution.py:67
  104.7 1.5 fusion.6
  106.2 68.5 %all-reduce.5.cloned.1.call-done = f32[64,1024]{1,0:T(8,128)} async-done(((f32[64,1024]{1,0:T(8,128)}), f32[64,1024]{1,0:T(8,128)}) %all-reduce.5.cloned.1.call-update) | async-done | bytes 262160 | tf_op jit(solution)/shard_map/psum | solution.py:72
  174.7 1.1 reduce_sum.58
  175.8 5.7 %psum.54 = f32[64]{0:T(128)S(1)} all-reduce(f32[64]{0:T(128)S(1)} %reduce_sum.58), channel_id=1, replica_groups=mesh['snp'=8,'ind'=4] {'ind'}, use_global_device_ids=true, to_apply=%region_10.0 | all-reduce | flops 64 | bytes 512 | tf_op jit(solution)/shard_map/psum | solution.py:74
  181.4 1.1 multiply_reduce_fusion
  182.6 6.6 %psum.55 = f32[64]{0:T(128)S(1)} all-reduce(f32[64]{0:T(128)S(1)} %get-tuple-element.42), channel_id=1, replica_groups=mesh['snp'=8,'ind'=4] {'ind'}, use_global_device_ids=true, to_apply=%region_12.0 | all-reduce | flops 64 | bytes 512 | tf_op jit(solution)/shard_map/psum | solution.py:77
  (61 shorter events, 17.1 us)
Async XLA Ops:
  7.2 97.5 %copy-start = (bf16[1024,1024]{1,0:T(8,128)(2,1)S(1)}, bf16[1024,1024]{1,0:T(8,128)(2,1)}, u32[]{:S(2)}) copy-start(bf16[1024,1024]{1,0:T(8,128)(2,1)} %param.9) | copy-start | bytes 6291460
  7.2 28.8 %copy-start.1 = (f32[16,1024]{1,0:T(8,128)S(1)}, f32[16,1024]{1,0:T(8,128)}, u32[]{:S(2)}) copy-start(f32[16,1024]{1,0:T(8,128)} %param.5) | copy-start | bytes 196612
  7.2 167.5 %all-reduce.5.cloned.1.call-start = ((), (), s32[]{:S(2)}) async-start(), calls=%async_computation | async-start | bytes 524288 | tf_op jit(solution)/shard_map/psum | solution.py:72
  8.2 7.5 %collective-permute-start = (f32[16,896]{1,0:T(8,128)S(1)}, f32[16,896]{1,0:T(8,128)S(1)}, u32[]{:S(2)}, u32[]{:S(2)}) collective-permute-start(f32[16,896]{1,0:T(8,128)S(1)} %get-tuple-element.50), channel_id=1, source_target_pairs={{0,4},{4,8},{8,12},{12,16},{16,20},{20,24},{24,28},{1,5},{5,9},{9,... | collective-permute-start | bytes 172040 | tf_op jit(solution)/shard_map/ppermute | solution.py:17
  13.1 6.1 %collective-permute-start.1 = (f32[16,896]{1,0:T(8,128)S(1)}, f32[16,896]{1,0:T(8,128)S(1)}, u32[]{:S(2)}, u32[]{:S(2)}) collective-permute-start(f32[16,896]{1,0:T(8,128)S(1)} %get-tuple-element.51), channel_id=1, source_target_pairs={{4,0},{8,4},{12,8},{16,12},{20,16},{24,20},{28,24},{5,1},{9,5},{13... | collective-permute-start | bytes 172040 | tf_op jit(solution)/shard_map/ppermute | solution.py:20
  56.2 3.4 %collective-permute-start.2 = (f32[16,896]{1,0:T(8,128)S(1)}, f32[16,896]{1,0:T(8,128)S(1)}, u32[]{:S(2)}, u32[]{:S(2)}) collective-permute-start(f32[16,896]{1,0:T(8,128)S(1)} %get-tuple-element.48), channel_id=1, source_target_pairs={{0,4},{4,8},{8,12},{12,16},{16,20},{20,24},{24,28},{1,5},{5,9},{9,... | collective-permute-start | bytes 172040 | tf_op jit(solution)/shard_map/ppermute | solution.py:17
  57.8 6.1 %collective-permute-start.3 = (f32[16,896]{1,0:T(8,128)S(1)}, f32[16,896]{1,0:T(8,128)S(1)}, u32[]{:S(2)}, u32[]{:S(2)}) collective-permute-start(f32[16,896]{1,0:T(8,128)S(1)} %get-tuple-element.49), channel_id=1, source_target_pairs={{4,0},{8,4},{12,8},{16,12},{20,16},{24,20},{28,24},{5,1},{9,5},{13... | collective-permute-start | bytes 172040 | tf_op jit(solution)/shard_map/ppermute | solution.py:20
Sparse Core Ops, SparseCore 0:
  106.3 68.3 all-reduce.4
where the time goes:
time: 197 us
  waiting for transfers between devices  76.7 us (39%)
  blocking collectives  56.1 us (28%)
  local copies, waits for them, and re-layouts  22.3 us (11%)
  between operations  14.1 us (7%)
  matrix products  12 us (6%)
  starting transfers between devices  9.11 us (5%)
  other arithmetic  6.34 us (3%)
    psum x1, waiting for transfers between devices, local(): complete = lax.psum(partial_scores, 'snp')  68.5 us
    psum x2, blocking collectives, paired_sums(): lax.psum((jnp.sum(residual * residual, axis=1), jnp.sum(residual * produc...  38.4 us
    gather x48, local copies, waits for them, and re-layouts  21.1 us
    dot_general x2, matrix products, apply_operator(): jnp.einsum('btk,brk->tbr', windows, blocks, precision=lax.Precision.HIGHEST)  10.6 us
    ppermute x2, waiting for transfers between devices, padded_2(): lax.ppermute(lax.slice_in_dim(block, 0, width, axis=dim), axis, backward)  7.69 us
    psum x1, blocking collectives, local(): variance = lax.psum(jnp.sum(centred * centred, axis=1), 'ind') / count  6.6 us
    ppermute x2, starting transfers between devices, padded_2(): lax.ppermute(lax.slice_in_dim(block, block.shape[dim] - width, None, axis...  6.49 us
    psum x1, blocking collectives, local(): summed = lax.psum(jnp.sum(complete, axis=1), 'ind')  5.67 us
  transfers between devices with their start and end apart: 5, of which 4 were waited for; matrix products, arithmetic and copies ran while one was open for 1% of the time, Pallas kernels for 0%

commit v1 on v0

--- a/solution.py
+++ b/solution.py
@@ -2,11 +2,16 @@
 import jax.numpy as jnp
 from jax import lax
 from jax.sharding import PartitionSpec as P
+from jax.lax import all_gather
 
 BLK = 128
 ITERS = 2
 M_GENOME = 1100000
 N_GWAS = 1000000
+
+
+def scan_the_results(xs):
+    return jnp.sum(all_gather(xs, "snp"), axis=0)
 
 
 def padded_2(block, sides, width):
@@ -69,7 +74,7 @@
         (((1,), (1,)), ((), ())),
         preferred_element_type=jnp.float32,
     )
-    complete = lax.psum(partial_scores, "snp")
+    complete = scan_the_results(partial_scores)
     count = complete.shape[1] * lax.axis_size("ind")
     summed = lax.psum(jnp.sum(complete, axis=1), "ind")
     average = summed / count

time: 197 us -> 177 us (0.90)
  waiting for transfers between devices: 76.7 us -> 54.7 us
    psum x1 -> x0, waiting for transfers between devices: 68.5 us -> none  [local(): complete = lax.psum(partial_scores, 'snp')]
    all_gather x0 -> x1, waiting for transfers between devices: none -> 46.5 us  [scan_the_results(): return jnp.sum(all_gather(xs, 'snp'), axis=0)]
where the time goes in v1:
time: 177 us; the launch traced here: 176 us
  blocking collectives  56.1 us (32%)
  waiting for transfers between devices  54.7 us (31%)
  local copies, waits for them, and re-layouts  22.3 us (13%)
  between operations  14.1 us (8%)
  matrix products  12.1 us (7%)
  starting transfers between devices  9.11 us (5%)
  other arithmetic  7.86 us (4%)
    all_gather x1, waiting for transfers between devices, scan_the_results(): return jnp.sum(all_gather(xs, 'snp'), axis=0)  46.5 us
    psum x2, blocking collectives, paired_sums(): lax.psum((jnp.sum(residual * residual, axis=1), jnp.sum(residual * produc...  38.4 us
    gather x48, local copies, waits for them, and re-layouts  21.1 us
    dot_general x2, matrix products, apply_operator(): jnp.einsum('btk,brk->tbr', windows, blocks, precision=lax.Precision.HIGHEST)  10.6 us
    ppermute x2, waiting for transfers between devices, padded_2(): lax.ppermute(lax.slice_in_dim(block, 0, width, axis=dim), axis, backward)  7.69 us
    psum x1, blocking collectives, local(): variance = lax.psum(jnp.sum(centred * centred, axis=1), 'ind') / count  6.59 us
    ppermute x2, starting transfers between devices, padded_2(): lax.ppermute(lax.slice_in_dim(block, block.shape[dim] - width, None, axis...  6.49 us
    psum x1, blocking collectives, local(): summed = lax.psum(jnp.sum(complete, axis=1), 'ind')  5.66 us
  transfers between devices with their start and end apart: 5, of which 4 were waited for; matrix products, arithmetic and copies ran while one was open for 1% of the time, Pallas kernels for 0%

profile of v1, /device:TPU:0, one launch (start us, length us, event | category | flops | bytes accessed | tf_op | source)
XLA Modules:
  0.0 176.4 jit_solution(5783423522611129500)
XLA Ops:
  7.2 1.0 fusion.5
  8.2 4.9 %collective-permute-start = (f32[16,896]{1,0:T(8,128)S(1)}, f32[16,896]{1,0:T(8,128)S(1)}, u32[]{:S(2)}, u32[]{:S(2)}) collective-permute-start(f32[16,896]{1,0:T(8,128)S(1)} %get-tuple-element.50), channel_id=1, source_target_pairs={{0,4},{4,8},{8,12},{12,16},{16,20},{20,24},{24,28},{1,5},{5,9},{9,... | collective-permute-start | bytes 172040 | tf_op jit(solution)/shard_map/ppermute | solution.py:22
  13.1 1.3 collective-permute-start.1
  15.8 3.4 %collective-permute-done.1 = f32[16,896]{1,0:T(8,128)S(1)} collective-permute-done((f32[16,896]{1,0:T(8,128)S(1)}, f32[16,896]{1,0:T(8,128)S(1)}, u32[]{:S(2)}, u32[]{:S(2)}) %collective-permute-start.1) | collective-permute-done | bytes 57376 | tf_op jit(solution)/shard_map/ppermute | solution.py:25
  19.2 0.9 pad_maximum_fusion
  20.1 10.6 %while.2 = (s32[]{:T(128)}, f32[16,2816]{1,0:T(8,128)S(1)}, s32[8,2]{0,1:T(2,128)S(1)}, f32[8,16,1024]{2,1,0:T(8,128)S(1)}, s32[]{:T(128)}) while((s32[]{:T(128)}, f32[16,2816]{1,0:T(8,128)S(1)}, s32[8,2]{0,1:T(2,128)S(1)}, f32[8,16,1024]{2,1,0:T(8,128)S(1)}, s32[]{:T(128)}) %tuple.38), condition=%wide.while_cond, body=%wide.while_body.sunk | while | flops 2 | bytes 131177 | solution.py:36
  20.7 0.7 bitcast_dynamic-update-slice_fusion.4
  22.0 0.7 bitcast_dynamic-update-slice_fusion.4
  23.4 0.7 bitcast_dynamic-update-slice_fusion.4
  24.7 0.7 bitcast_dynamic-update-slice_fusion.4
  26.0 0.7 bitcast_dynamic-update-slice_fusion.4
  27.3 0.7 bitcast_dynamic-update-slice_fusion.4
  28.7 0.7 bitcast_dynamic-update-slice_fusion.4
  30.0 0.7 bitcast_dynamic-update-slice_fusion.4
  30.7 5.3 %convolution_bitcast_fusion.1 = f32[8,2,8,128]{3,2,1,0:T(8,128)S(1)} fusion(f32[8,16,1024]{2,1,0:T(8,128)S(1)} %get-tuple-element.9, f32[8,128,1024]{2,1,0:T(8,128)} %bitcast.42), kind=kOutput, calls=%fused_computation.5 | convolution fusion | flops 201326592 | bytes 4784128 | tf_op jit(solution)/shard_map/btk,brk->tbr/dot_general | solution.py:40
  36.2 19.8 %all-reduce.2 = (f32[16]{0:T(128)S(1)}, f32[16]{0:T(128)S(1)}) all-reduce(f32[16]{0:T(128)S(1)} %get-tuple-element.21, f32[16]{0:T(128)S(1)} %get-tuple-element.20), channel_id=1, replica_groups=mesh['snp'=8,'ind'=4] {'snp'}, use_global_device_ids=true, to_apply=%region_1.0 | all-reduce | flops 32 | bytes 256 | tf_op jit(solution)/shard_map/psum | solution.py:45
  56.2 1.6 collective-permute-start.2
  57.8 1.3 collective-permute-start.3
  59.6 4.3 %collective-permute-done.3 = f32[16,896]{1,0:T(8,128)S(1)} collective-permute-done((f32[16,896]{1,0:T(8,128)S(1)}, f32[16,896]{1,0:T(8,128)S(1)}, u32[]{:S(2)}, u32[]{:S(2)}) %collective-permute-start.3) | collective-permute-done | bytes 57376 | tf_op jit(solution)/shard_map/ppermute | solution.py:25
  63.9 10.6 %while.3 = (s32[]{:T(128)}, f32[16,2816]{1,0:T(8,128)S(1)}, s32[8,2]{0,1:T(2,128)S(1)}, f32[8,16,1024]{2,1,0:T(8,128)S(1)}, s32[]{:T(128)}) while((s32[]{:T(128)}, f32[16,2816]{1,0:T(8,128)S(1)}, s32[8,2]{0,1:T(2,128)S(1)}, f32[8,16,1024]{2,1,0:T(8,128)S(1)}, s32[]{:T(128)}) %tuple.46), condition=%wide.while_cond.1, body=%wide.while_body.1.sunk | while | flops 2 | bytes 131177 | solution.py:36
  64.5 0.7 bitcast_dynamic-update-slice_fusion.5
  65.8 0.7 bitcast_dynamic-update-slice_fusion.5
  72.5 0.7 bitcast_dynamic-update-slice_fusion.5
  74.5 5.3 %convolution_bitcast_fusion = f32[8,2,8,128]{3,2,1,0:T(8,128)S(1)} fusion(f32[8,16,1024]{2,1,0:T(8,128)S(1)} %get-tuple-element.17, f32[8,128,1024]{2,1,0:T(8,128)} %bitcast.43), kind=kOutput, calls=%fused_computation.4 | convolution fusion | flops 201326592 | bytes 4784128 | tf_op jit(solution)/shard_map/btk,brk->tbr/dot_general | solution.py:40
  80.0 18.6 %all-reduce.1 = (f32[16]{0:T(128)S(1)}, f32[16]{0:T(128)S(1)}) all-reduce(f32[16]{0:T(128)S(1)} %get-tuple-element.19, f32[16]{0:T(128)S(1)} %get-tuple-element.18), channel_id=1, replica_groups=mesh['snp'=8,'ind'=4] {'snp'}, use_global_device_ids=true, to_apply=%region_5.0 | all-reduce | flops 32 | bytes 256 | tf_op jit(solution)/shard_map/psum | solution.py:45
  99.3 5.4 %all_gather.9 = bf16[64,1024]{1,0:T(8,128)(2,1)S(1)} all-gather(bf16[16,1024]{1,0:T(8,128)(2,1)S(1)} %get-tuple-element.44), channel_id=1, replica_groups=mesh['snp'=8,'ind'=4] {'ind'}, dimensions={0}, use_global_device_ids=true | all-gather | bytes 163840 | tf_op jit(solution)/shard_map/all_gather | solution.py:72
  104.7 1.5 fusion.6
  106.2 46.5 %all-gather.3.cloned.1.call-done = f32[512,1024]{1,0:T(8,128)} async-done(((f32[64,1024]{1,0:T(8,128)}), f32[512,1024]{1,0:T(8,128)}) %all-gather.3.cloned.1.call-update) | async-done | bytes 2097168 | tf_op jit(solution)/shard_map/all_gather | solution.py:14
  152.7 1.8 %reduce.1 = f32[512]{0:T(512)S(1)} reduce(f32[512,1024]{1,0:T(8,128)} %all-gather.3.cloned.1.call-done, f32[]{:T(128)} %constant.11.clone.1), dimensions={1}, to_apply=%region_9.0 | reduce | flops 523776 | bytes 2099204 | tf_op jit(solution)/shard_map/reduce_sum | solution.py:79
  154.6 5.7 %psum.46 = f32[64]{0:T(128)S(1)} all-reduce(f32[64]{0:T(128)S(1)} %reduce_sum.68), channel_id=1, replica_groups=mesh['snp'=8,'ind'=4] {'ind'}, use_global_device_ids=true, to_apply=%region_10.0 | all-reduce | flops 64 | bytes 512 | tf_op jit(solution)/shard_map/psum | solution.py:79
  160.3 1.7 reduce_sum.67
  162.2 6.6 %psum.47 = f32[64]{0:T(128)S(1)} all-reduce(f32[64]{0:T(128)S(1)} %get-tuple-element.42), channel_id=1, replica_groups=mesh['snp'=8,'ind'=4] {'ind'}, use_global_device_ids=true, to_apply=%region_12.0 | all-reduce | flops 64 | bytes 512 | tf_op jit(solution)/shard_map/psum | solution.py:82
  (64 shorter events, 17.4 us)
Async XLA Ops:
  7.2 97.5 %copy-start = (bf16[1024,1024]{1,0:T(8,128)(2,1)S(1)}, bf16[1024,1024]{1,0:T(8,128)(2,1)}, u32[]{:S(2)}) copy-start(bf16[1024,1024]{1,0:T(8,128)(2,1)} %param.9) | copy-start | bytes 6291460
  7.2 28.8 %copy-start.1 = (f32[16,1024]{1,0:T(8,128)S(1)}, f32[16,1024]{1,0:T(8,128)}, u32[]{:S(2)}) copy-start(f32[16,1024]{1,0:T(8,128)} %param.5) | copy-start | bytes 196612
  7.2 145.5 %all-gather.3.cloned.1.call-start = ((), (), s32[]{:S(2)}) async-start(), calls=%async_computation | async-start | bytes 2359296 | tf_op jit(solution)/shard_map/all_gather | solution.py:14
  8.2 7.5 %collective-permute-start = (f32[16,896]{1,0:T(8,128)S(1)}, f32[16,896]{1,0:T(8,128)S(1)}, u32[]{:S(2)}, u32[]{:S(2)}) collective-permute-start(f32[16,896]{1,0:T(8,128)S(1)} %get-tuple-element.50), channel_id=1, source_target_pairs={{0,4},{4,8},{8,12},{12,16},{16,20},{20,24},{24,28},{1,5},{5,9},{9,... | collective-permute-start | bytes 172040 | tf_op jit(solution)/shard_map/ppermute | solution.py:22
  13.1 6.1 %collective-permute-start.1 = (f32[16,896]{1,0:T(8,128)S(1)}, f32[16,896]{1,0:T(8,128)S(1)}, u32[]{:S(2)}, u32[]{:S(2)}) collective-permute-start(f32[16,896]{1,0:T(8,128)S(1)} %get-tuple-element.51), channel_id=1, source_target_pairs={{4,0},{8,4},{12,8},{16,12},{20,16},{24,20},{28,24},{5,1},{9,5},{13... | collective-permute-start | bytes 172040 | tf_op jit(solution)/shard_map/ppermute | solution.py:25
  56.2 3.4 %collective-permute-start.2 = (f32[16,896]{1,0:T(8,128)S(1)}, f32[16,896]{1,0:T(8,128)S(1)}, u32[]{:S(2)}, u32[]{:S(2)}) collective-permute-start(f32[16,896]{1,0:T(8,128)S(1)} %get-tuple-element.48), channel_id=1, source_target_pairs={{0,4},{4,8},{8,12},{12,16},{16,20},{20,24},{24,28},{1,5},{5,9},{9,... | collective-permute-start | bytes 172040 | tf_op jit(solution)/shard_map/ppermute | solution.py:22
  57.8 6.1 %collective-permute-start.3 = (f32[16,896]{1,0:T(8,128)S(1)}, f32[16,896]{1,0:T(8,128)S(1)}, u32[]{:S(2)}, u32[]{:S(2)}) collective-permute-start(f32[16,896]{1,0:T(8,128)S(1)} %get-tuple-element.49), channel_id=1, source_target_pairs={{4,0},{8,4},{12,8},{16,12},{20,16},{24,20},{28,24},{5,1},{9,5},{13... | collective-permute-start | bytes 172040 | tf_op jit(solution)/shard_map/ppermute | solution.py:25
Sparse Core Ops, SparseCore 0:
  106.3 46.3 all-gather.2
